TPU v7x, 512 devices: a whole 4x4x16 slice. The times are simulated.
512 devices in a mesh: lon: 64 (over x, y, z_hi, core), lat: 8 (over z_lo).
Axes of the slice: x: 4, y: 4, z: 16 (z_hi: 2, z_lo: 8; z = z_hi * 8 + z_lo), core: 2. Of those that a mesh axis runs over, the one named last changes fastest.
Arguments:
- potential_heat: float32 [4, 768, 8192], P(None, 'lat', 'lon'), may hold values from -6 to 6
- salt_anomaly_field: float32 [4, 768, 8192], P(None, 'lat', 'lon'), may hold values from -6 to 6
- zonal_current: float32 [4, 768, 8192], P(None, 'lat', 'lon'), may hold values from -6 to 6
- meridional_current: float32 [4, 768, 8192], P(None, 'lat', 'lon'), may hold values from -6 to 6
- water_indicator: int32 [4, 768, 8192], P(None, 'lat', 'lon'), may hold values 0 or 1
- floor_layer_index: int32 [768, 8192], P('lat', 'lon'), may hold values from 0 to 3
- zonal_spacing: float32 [768, 8192], P('lat', 'lon'), may hold values from 0.7 to 1.4
- meridional_spacing: float32 [768, 8192], P('lat', 'lon'), may hold values from 0.7 to 1.4
- planetary_rotation_factor: float32 [768, 8192], P('lat', 'lon'), may hold values from 0.3 to 1.5
- horizontal_eddy_coefficient: float32 [768, 8192], P('lat', 'lon'), may hold values from 0.05 to 0.25
- diapycnal_diffusivity: float32 [3, 768, 8192], P(None, 'lat', 'lon'), may hold values from 0.02 to 0.5
- layer_height: float32 [4], replicated, may hold values from 0.7 to 1.4
Outputs:
- new_temperature: float32 [4, 768, 8192], P(None, 'lat', 'lon')
- new_salinity: float32 [4, 768, 8192], P(None, 'lat', 'lon')
- new_zonal: float32 [4, 768, 8192], P(None, 'lat', 'lon')
- new_meridional: float32 [4, 768, 8192], P(None, 'lat', 'lon')
All inputs are finite; a program needn't handle non-finite values. No bound on the sum of `water_indicator` on one device may be relied on, other than what follows from the above.
Results may differ from a plain program's by a relative error of at most 0.0003.
Values sent between devices are 32-bit elements; how exact they have to be, the bound alone decides.
No kernel may reach another device: no remote copies, remote signals or barrier semaphores. Data moves between devices by JAX's collectives and lax.ppermute only.
A program may use at most 64 MiB of HBM per device.

v0:
```python
import jax
import jax.numpy as jnp
from jax import lax
from jax.sharding import PartitionSpec as P

TIME_STEP = 0.25
EXPANSION = 0.2
CONTRACTION = 0.8
BOTTOM_DRAG = 1.0


def with_halo(value, sides, width, wrap):
    for axis, dim in sides:
        size, length = (lax.axis_size(axis), value.shape[dim])
        up = [(i, (i + 1) % size) for i in range(size if wrap else size - 1)]
        down = [(j, i) for i, j in up]
        last = lax.slice_in_dim(value, length - width, length, axis=dim)
        leading = lax.slice_in_dim(value, 0, width, axis=dim)
        before = lax.ppermute(last, axis, up)
        after = lax.ppermute(leading, axis, down)
        value = jnp.concatenate([before, value, after], axis=dim)
    return value


def pressure(temp_part, salt_part, layer_height):
    layer_mass = (CONTRACTION * salt_part - EXPANSION * temp_part) * layer_height[:, None, None]
    return jnp.cumsum(layer_mass, axis=0) - 0.5 * layer_mass


def mix_vertically(fields, water_share, diapycnal_diffusivity, layer_height):
    contrast = fields[:, 1:] - fields[:, :-1]
    fluxes = diapycnal_diffusivity * (water_share[1:] * water_share[:-1]) * contrast
    boundary = jnp.zeros_like(fluxes[:, :1])
    flux_below = jnp.concatenate([fluxes, boundary], axis=1)
    flux_above = jnp.concatenate([boundary, fluxes], axis=1)
    return (flux_below - flux_above) / (layer_height * layer_height)[None, :, None, None]


def advance(
    central,
    eastern,
    western,
    northern,
    southern,
    at_bottom,
    zonal_spacing,
    meridional_spacing,
    planetary_rotation_factor,
    horizontal_eddy_coefficient,
    diapycnal_diffusivity,
    layer_height,
):
    water_share = central[4]
    fields = central[:4]
    weight_east = water_share * eastern[4]
    weight_west = water_share * western[4]
    weight_north = water_share * northern[4]
    weight_south = water_share * southern[4]
    diffusion = horizontal_eddy_coefficient * (
        (weight_east * (eastern[:4] - fields) + weight_west * (western[:4] - fields))
        / (zonal_spacing * zonal_spacing)
        + (weight_north * (northern[:4] - fields) + weight_south * (southern[:4] - fields))
        / (meridional_spacing * meridional_spacing)
    )
    zonal = fields[2]
    merid = fields[3]
    advection = -(
        zonal * (eastern[:4] - western[:4]) * (0.5 / zonal_spacing)
        + merid * (northern[:4] - southern[:4]) * (0.5 / meridional_spacing)
    )
    pressure_east = pressure(eastern[0], eastern[1], layer_height)
    pressure_west = pressure(western[0], western[1], layer_height)
    pressure_north = pressure(northern[0], northern[1], layer_height)
    pressure_south = pressure(southern[0], southern[1], layer_height)
    gradient_x = -(pressure_east - pressure_west) * (0.5 / zonal_spacing)
    gradient_y = -(pressure_north - pressure_south) * (0.5 / meridional_spacing)
    mixing = mix_vertically(fields, water_share, diapycnal_diffusivity, layer_height)
    tendency = advection + diffusion + mixing
    tend_zonal = (
        tendency[2]
        + planetary_rotation_factor * merid
        + gradient_x
        - BOTTOM_DRAG * at_bottom * zonal
    )
    tend_merid = (
        tendency[3]
        - planetary_rotation_factor * zonal
        + gradient_y
        - BOTTOM_DRAG * at_bottom * merid
    )
    tendency = jnp.stack([tendency[0], tendency[1], tend_zonal, tend_merid])
    updated = water_share * (fields + TIME_STEP * tendency)
    return jnp.concatenate([updated, water_share[None]], axis=0)


def fold_ghost(top_row):
    fold_sign = jnp.array([1.0, 1.0, -1.0, -1.0, 1.0], jnp.float32).reshape(5, 1, 1)
    row_width = top_row.shape[2]
    gathered = lax.all_gather(top_row, "lon", axis=2, tiled=True)
    partner = lax.axis_size("lon") - 1 - lax.axis_index("lon")
    mirrored = lax.dynamic_slice_in_dim(gathered, partner * row_width, row_width, 2)
    return mirrored[:, :, ::-1] * fold_sign


def shards(
    potential_heat,
    salt_anomaly_field,
    zonal_current,
    meridional_current,
    water_indicator,
    floor_layer_index,
    zonal_spacing,
    meridional_spacing,
    planetary_rotation_factor,
    horizontal_eddy_coefficient,
    diapycnal_diffusivity,
    layer_height,
):
    water_share = water_indicator.astype(jnp.float32)
    combined_tracers = jnp.stack(
        [
            potential_heat * water_share,
            salt_anomaly_field * water_share,
            zonal_current * water_share,
            meridional_current * water_share,
            water_share,
        ]
    )
    levels = combined_tracers.shape[1]
    is_top = lax.axis_index("lat") == lax.axis_size("lat") - 1
    at_bottom = (
        lax.broadcasted_iota(jnp.int32, (levels, 1, 1), 0) == floor_layer_index[None]
    ).astype(jnp.float32)
    for step_index in range(2):
        lon_padded = with_halo(combined_tracers, (("lon", 3),), 1, True)
        lat_padded = with_halo(combined_tracers, (("lat", 2),), 1, False)
        ghost_row = fold_ghost(combined_tracers[:, :, -1, :])
        north_rim = jnp.where(is_top, ghost_row, lat_padded[:, :, -1, :])
        northern = jnp.concatenate([lat_padded[:, :, 2:-1, :], north_rim[:, :, None, :]], axis=2)
        southern = lat_padded[:, :, :-2, :]
        eastern = lon_padded[..., 2:]
        western = lon_padded[..., :-2]
        combined_tracers = advance(
            combined_tracers,
            eastern,
            western,
            northern,
            southern,
            at_bottom,
            zonal_spacing,
            meridional_spacing,
            planetary_rotation_factor,
            horizontal_eddy_coefficient,
            diapycnal_diffusivity,
            layer_height,
        )
    return (combined_tracers[0], combined_tracers[1], combined_tracers[2], combined_tracers[3])


def solution(mesh):
    return jax.shard_map(
        shards,
        mesh=mesh,
        in_specs=(
            P(None, "lat", "lon"),
            P(None, "lat", "lon"),
            P(None, "lat", "lon"),
            P(None, "lat", "lon"),
            P(None, "lat", "lon"),
            P("lat", "lon"),
            P("lat", "lon"),
            P("lat", "lon"),
            P("lat", "lon"),
            P("lat", "lon"),
            P(None, "lat", "lon"),
            P(),
        ),
        out_specs=(
            P(None, "lat", "lon"),
            P(None, "lat", "lon"),
            P(None, "lat", "lon"),
            P(None, "lat", "lon"),
        ),
        check_vma=False,
    )
```

profile of v0, /device:TPU:96, one launch (start us, length us, event | category | flops | bytes accessed | tf_op | source)
XLA Modules:
  0.0 402.4 jit_solution(17297029420401216242)
XLA Ops:
  0.7 1.1 constant_dynamic-update-slice_fusion.4
  1.8 1.1 constant_dynamic-update-slice_fusion.3
  2.9 1.1 constant_dynamic-update-slice_fusion.2
  4.7 2.0 collective-permute-start.2
  6.8 5.0 %collective-permute-start.3 = (f32[5,4,1,128]{3,2,1,0:T(1,128)}, f32[5,4,1,128]{3,2,1,0:T(1,128)S(1)}, u32[]{:S(2)}, u32[]{:S(2)}) collective-permute-start(f32[5,4,1,128]{3,2,1,0:T(1,128)} %get-tuple-element.27), channel_id=1, source_target_pairs={{0,1},{1,2},{2,3},{3,4},{4,5},{5,6},{6,7},{8,9},{9,10},{10,11},{11... | collective-permute-start | bytes 30728 | tf_op jit(solution)/shard_map/ppermute | solution.py:19
  11.8 1.3 fusion.149
  13.1 2.2 copy.83
  15.2 16.5 %collective-permute-start = (f32[5,4,96,1]{2,1,3,0:T(4,128)}, f32[5,4,96,1]{2,1,3,0:T(4,128)}, u32[]{:S(2)}, u32[]{:S(2)}) collective-permute-start(f32[5,4,96,1]{2,1,3,0:T(4,128)} %copy.83), channel_id=1, source_target_pairs={{8,0},{16,8},{24,16},{32,24},{40,32},{48,40},{56,48},{64,56},{72,6... | collective-permute-start | bytes 23048 | tf_op jit(solution)/shard_map/ppermute | solution.py:20
  32.1 1.9 collective-permute-start.1
  34.1 150.4 %all-gather = f32[5,4,1,8192]{3,2,1,0:T(1,128)S(1)} all-gather(f32[5,4,1,128]{3,2,1,0:T(1,128)} %get-tuple-element.27), channel_id=2, replica_groups=mesh['lon'=64,'lat'=8] {'lon'}, dimensions={3}, use_global_device_ids=true | all-gather | bytes 665600 | tf_op jit(solution)/shard_map/all_gather | solution.py:99
  187.7 1.1 copy.86
  189.7 2.0 copy.84
  192.6 1.4 fusion.74
  194.3 1.3 divide_add_fusion.1
  197.4 1.3 fusion.22
  198.8 164.6 %all-gather.1 = f32[5,4,1,8192]{3,2,1,0:T(1,128)} all-gather(f32[5,4,1,128]{3,2,1,0:T(1,128)S(1)} %get-tuple-element.23), channel_id=3, replica_groups=mesh['lon'=64,'lat'=8] {'lon'}, dimensions={3}, use_global_device_ids=true | all-gather | bytes 665600 | tf_op jit(solution)/shard_map/all_gather | solution.py:99
  363.4 1.9 collective-permute-start.7
  366.9 1.5 copy.91
  368.5 2.3 collective-permute-start.5
  371.1 16.2 %collective-permute-start.4 = (f32[5,4,96,1]{2,1,3,0:T(4,128)S(1)}, f32[5,4,96,1]{2,1,3,0:T(4,128)S(1)}, u32[]{:S(2)}, u32[]{:S(2)}) collective-permute-start(f32[5,4,96,1]{2,1,3,0:T(4,128)S(1)} %copy.89), channel_id=1, source_target_pairs={{8,0},{16,8},{24,16},{32,24},{40,32},{48,40},{56,48},{64,56},{72,6... | collective-permute-start | bytes 23048 | tf_op jit(solution)/shard_map/ppermute | solution.py:20
  388.1 3.9 collective-permute-start.6
  393.4 1.3 copy.90
  394.7 1.9 pad_maximum_fusion
  396.8 1.0 copy-done.1
  (144 shorter events, 16.6 us)
Async XLA Ops:
  0.6 3.4 copy-start.2
  0.6 3.4 copy-start.41
  1.8 182.9 %copy-start.4 = (f32[1,4,96,128]{3,2,1,0:T(8,128)}, f32[1,4,96,128]{3,2,1,0:T(8,128)S(1)}, u32[]{:S(2)}) copy-start(f32[1,4,96,128]{3,2,1,0:T(8,128)S(1)} %get-tuple-element.11) | copy-start | bytes 589828
  2.9 181.7 %copy-start.7 = (f32[1,4,96,128]{3,2,1,0:T(8,128)}, f32[1,4,96,128]{3,2,1,0:T(8,128)S(1)}, u32[]{:S(2)}) copy-start(f32[1,4,96,128]{3,2,1,0:T(8,128)S(1)} %get-tuple-element.9) | copy-start | bytes 589828
  4.7 187.0 %collective-permute-start.2 = (f32[5,4,1,128]{3,1,0,2:T(4,128)}, f32[5,4,1,128]{3,1,0,2:T(4,128)}, u32[]{:S(2)}, u32[]{:S(2)}) collective-permute-start(f32[5,4,1,128]{3,1,0,2:T(4,128)} %bitcast.37), channel_id=1, source_target_pairs={{1,0},{2,1},{3,2},{4,3},{5,4},{6,5},{7,6},{9,8},{10,9},{11,10},{12... | collective-permute-start | bytes 30728 | tf_op jit(solution)/shard_map/ppermute | solution.py:20
  6.8 185.8 %collective-permute-start.3 = (f32[5,4,1,128]{3,2,1,0:T(1,128)}, f32[5,4,1,128]{3,2,1,0:T(1,128)S(1)}, u32[]{:S(2)}, u32[]{:S(2)}) collective-permute-start(f32[5,4,1,128]{3,2,1,0:T(1,128)} %get-tuple-element.27), channel_id=1, source_target_pairs={{0,1},{1,2},{2,3},{3,4},{4,5},{5,6},{6,7},{8,9},{9,10},{10,11},{11... | collective-permute-start | bytes 30728 | tf_op jit(solution)/shard_map/ppermute | solution.py:19
  13.1 171.5 %copy-start.42 = (f32[3,96,128]{2,1,0:T(8,128)S(1)}, f32[3,96,128]{2,1,0:T(8,128)}, u32[]{:S(2)}) copy-start(f32[3,96,128]{2,1,0:T(8,128)} %param.24) | copy-start | bytes 442372
  15.2 174.5 %collective-permute-start = (f32[5,4,96,1]{2,1,3,0:T(4,128)}, f32[5,4,96,1]{2,1,3,0:T(4,128)}, u32[]{:S(2)}, u32[]{:S(2)}) collective-permute-start(f32[5,4,96,1]{2,1,3,0:T(4,128)} %copy.83), channel_id=1, source_target_pairs={{8,0},{16,8},{24,16},{32,24},{40,32},{48,40},{56,48},{64,56},{72,6... | collective-permute-start | bytes 23048 | tf_op jit(solution)/shard_map/ppermute | solution.py:20
  32.1 155.5 %collective-permute-start.1 = (f32[5,4,96,1]{2,1,3,0:T(4,128)S(1)}, f32[5,4,96,1]{2,1,3,0:T(4,128)}, u32[]{:S(2)}, u32[]{:S(2)}) collective-permute-start(f32[5,4,96,1]{2,1,3,0:T(4,128)S(1)} %copy.85), channel_id=1, source_target_pairs={{0,8},{8,16},{16,24},{24,32},{32,40},{40,48},{48,56},{56,64},{64,7... | collective-permute-start | bytes 23048 | tf_op jit(solution)/shard_map/ppermute | solution.py:19
  184.6 1.7 copy-start.21
  184.7 2.4 copy-start.43
  192.6 1.6 copy-start.19
  192.6 1.6 copy-start.23
  192.6 1.6 copy-start.25
  192.6 1.6 copy-start.35
  198.7 166.6 %copy-start.22 = (f32[3,96,128]{2,1,0:T(8,128)S(1)}, f32[3,96,128]{2,1,0:T(8,128)}, u32[]{:S(2)}) copy-start(f32[3,96,128]{2,1,0:T(8,128)} %copy-done.21) | copy-start | bytes 442372
  363.4 33.4 %collective-permute-start.7 = (f32[5,4,1,128]{3,2,1,0:T(1,128)S(1)}, f32[5,4,1,128]{3,2,1,0:T(1,128)S(1)}, u32[]{:S(2)}, u32[]{:S(2)}) collective-permute-start(f32[5,4,1,128]{3,2,1,0:T(1,128)S(1)} %get-tuple-element.23), channel_id=1, source_target_pairs={{0,1},{1,2},{2,3},{3,4},{4,5},{5,6},{6,7},{8,9},{9,10},{10,11},{11... | collective-permute-start | bytes 30728 | tf_op jit(solution)/shard_map/ppermute | solution.py:19
  368.5 23.6 %collective-permute-start.5 = (f32[5,4,96,1]{2,1,3,0:T(4,128)S(1)}, f32[5,4,96,1]{2,1,3,0:T(4,128)S(1)}, u32[]{:S(2)}, u32[]{:S(2)}) collective-permute-start(f32[5,4,96,1]{2,1,3,0:T(4,128)S(1)} %copy.91), channel_id=1, source_target_pairs={{0,8},{8,16},{16,24},{24,32},{32,40},{40,48},{48,56},{56,64},{64,7... | collective-permute-start | bytes 23048 | tf_op jit(solution)/shard_map/ppermute | solution.py:19
  371.1 22.3 %collective-permute-start.4 = (f32[5,4,96,1]{2,1,3,0:T(4,128)S(1)}, f32[5,4,96,1]{2,1,3,0:T(4,128)S(1)}, u32[]{:S(2)}, u32[]{:S(2)}) collective-permute-start(f32[5,4,96,1]{2,1,3,0:T(4,128)S(1)} %copy.89), channel_id=1, source_target_pairs={{8,0},{16,8},{24,16},{32,24},{40,32},{48,40},{56,48},{64,56},{72,6... | collective-permute-start | bytes 23048 | tf_op jit(solution)/shard_map/ppermute | solution.py:20
  388.1 8.5 %collective-permute-start.6 = (f32[5,4,1,128]{3,2,1,0:T(1,128)S(1)}, f32[5,4,1,128]{3,2,1,0:T(1,128)S(1)}, u32[]{:S(2)}, u32[]{:S(2)}) collective-permute-start(f32[5,4,1,128]{3,2,1,0:T(1,128)S(1)} %get-tuple-element.22), channel_id=1, source_target_pairs={{1,0},{2,1},{3,2},{4,3},{5,4},{6,5},{7,6},{9,8},{10,9},{11,10},{12... | collective-permute-start | bytes 30728 | tf_op jit(solution)/shard_map/ppermute | solution.py:20
  394.7 1.9 copy-start.46
  397.9 1.6 copy-start.34
  397.9 1.6 copy-start.36
  397.9 1.6 copy-start.38
  (33 other events, 42.2 us)
where the time goes:
time: 403 us; the launch traced here: 402 us
  blocking collectives  315 us (78%)
  starting transfers between devices  49.8 us (12%)
  other arithmetic  18.4 us (5%)
  local copies, waits for them, and re-layouts  17.8 us (4%)
    all_gather x2, blocking collectives, fold_ghost(): gathered = lax.all_gather(top_row, 'lon', axis=2, tiled=True)  315 us
    ppermute x4, starting transfers between devices, with_halo(): after = lax.ppermute(leading, axis, down)  38.7 us
    ppermute x4, starting transfers between devices, with_halo(): before = lax.ppermute(last, axis, up)  11.1 us
  transfers between devices with their start and end apart: 8, of which 0 were waited for; matrix products, arithmetic and copies ran while one was open for 5% of the time, Pallas kernels for 0%

commit v1 on v0

--- a/solution.py
+++ b/solution.py
@@ -7,6 +7,11 @@
 EXPANSION = 0.2
 CONTRACTION = 0.8
 BOTTOM_DRAG = 1.0
+
+
+def gather_over(x, axis, d):
+    sent = jnp.stack([x] * lax.axis_size(axis))
+    return jnp.concatenate(lax.all_to_all(sent, axis, 0, 0), axis=d)
 
 
 def with_halo(value, sides, width, wrap):
@@ -96,7 +101,7 @@
 def fold_ghost(top_row):
     fold_sign = jnp.array([1.0, 1.0, -1.0, -1.0, 1.0], jnp.float32).reshape(5, 1, 1)
     row_width = top_row.shape[2]
-    gathered = lax.all_gather(top_row, "lon", axis=2, tiled=True)
+    gathered = gather_over(top_row, "lon", 2)
     partner = lax.axis_size("lon") - 1 - lax.axis_index("lon")
     mirrored = lax.dynamic_slice_in_dim(gathered, partner * row_width, row_width, 2)
     return mirrored[:, :, ::-1] * fold_sign

time: 403 us -> 154 us (0.38)
  the two profiles are of different devices: /device:TPU:96 before, /device:TPU:32 now
where the time goes in v1:
time: 154 us; the launch traced here: 153 us
  starting transfers between devices  74.4 us (48%)
  waiting for transfers between devices  26.9 us (17%)
  local copies, waits for them, and re-layouts  25.6 us (17%)
  other arithmetic  24.7 us (16%)
    ppermute x4, starting transfers between devices, with_halo(): after = lax.ppermute(leading, axis, down)  38.9 us
    ppermute x4, waiting for transfers between devices, with_halo(): before = lax.ppermute(last, axis, up)  26.9 us
    all_to_all x2, starting transfers between devices, gather_over(): return jnp.concatenate(lax.all_to_all(sent, axis, 0, 0), axis=d)  26 us
    ppermute x4, starting transfers between devices, with_halo(): before = lax.ppermute(last, axis, up)  9.51 us
    another operation x8, other arithmetic, pressure(): return jnp.cumsum(layer_mass, axis=0) - 0.5 * layer_mass  4.84 us
    unnamed x104, local copies, waits for them, and re-layouts  4.25 us
    ppermute x2, local copies, waits for them, and re-layouts, with_halo(): after = lax.ppermute(leading, axis, down)  4.08 us
    add x2, other arithmetic, advance(): tendency = advection + diffusion + mixing  3.98 us
  transfers between devices with their start and end apart: 10, of which 2 were waited for; matrix products, arithmetic and copies ran while one was open for 18% of the time, Pallas kernels for 0%

profile of v1, /device:TPU:32, one launch (start us, length us, event | category | flops | bytes accessed | tf_op | source)
XLA Modules:
  0.0 153.0 jit_solution(6646809257808822381)
XLA Ops:
  4.7 1.6 %stack.49 = f32[64,5,4,128]{3,2,1,0:T(4,128)} broadcast(f32[5,4,128]{2,1,0:T(4,128)} %bitcast.5), dimensions={1,2,3} | broadcast | bytes 665600 | tf_op jit(solution)/shard_map/stack | solution.py:13
  6.4 20.5 %all-to-all-start = ((f32[64,5,4,128]{3,2,1,0:T(4,128)}), f32[64,5,4,128]{3,2,1,0:T(4,128)}, u32[]{:S(2)}, u32[]{:S(2)}) async-start(f32[64,5,4,128]{3,2,1,0:T(4,128)} %stack.49), calls=%async_computation | async-start | bytes 1310720 | tf_op jit(solution)/shard_map/all_to_all | solution.py:14
  26.9 2.9 %collective-permute-start.3 = (f32[5,4,1,128]{3,2,1,0:T(1,128)}, f32[5,4,1,128]{3,2,1,0:T(1,128)S(1)}, u32[]{:S(2)}, u32[]{:S(2)}) collective-permute-start(f32[5,4,1,128]{3,2,1,0:T(1,128)} %get-tuple-element.27), channel_id=1, source_target_pairs={{0,1},{1,2},{2,3},{3,4},{4,5},{5,6},{6,7},{8,9},{9,10},{10,11},{11... | collective-permute-start | bytes 30728 | tf_op jit(solution)/shard_map/ppermute | solution.py:24
  29.8 2.9 %collective-permute-start.2 = (f32[5,4,1,128]{3,1,0,2:T(4,128)}, f32[5,4,1,128]{3,1,0,2:T(4,128)}, u32[]{:S(2)}, u32[]{:S(2)}) collective-permute-start(f32[5,4,1,128]{3,1,0,2:T(4,128)} %bitcast.39), channel_id=1, source_target_pairs={{1,0},{2,1},{3,2},{4,3},{5,4},{6,5},{7,6},{9,8},{10,9},{11,10},{12... | collective-permute-start | bytes 30728 | tf_op jit(solution)/shard_map/ppermute | solution.py:25
  32.8 1.3 fusion.149
  34.1 2.2 %copy.83 = f32[5,4,96,1]{2,1,3,0:T(4,128)} copy(f32[5,4,96,1]{3,2,1,0:T(8,128)} %get-tuple-element.25) | data formatting | bytes 15360 | tf_op jit(solution)/shard_map/slice | solution.py:23
  36.2 15.8 %collective-permute-start = (f32[5,4,96,1]{2,1,3,0:T(4,128)}, f32[5,4,96,1]{2,1,3,0:T(4,128)}, u32[]{:S(2)}, u32[]{:S(2)}) collective-permute-start(f32[5,4,96,1]{2,1,3,0:T(4,128)} %copy.83), channel_id=1, source_target_pairs={{8,0},{16,8},{24,16},{32,24},{40,32},{48,40},{56,48},{64,56},{72,6... | collective-permute-start | bytes 23048 | tf_op jit(solution)/shard_map/ppermute | solution.py:25
  52.4 1.9 %collective-permute-start.1 = (f32[5,4,96,1]{2,1,3,0:T(4,128)S(1)}, f32[5,4,96,1]{2,1,3,0:T(4,128)}, u32[]{:S(2)}, u32[]{:S(2)}) collective-permute-start(f32[5,4,96,1]{2,1,3,0:T(4,128)S(1)} %copy.85), channel_id=1, source_target_pairs={{0,8},{8,16},{16,24},{24,32},{32,40},{40,48},{48,56},{56,64},{64,7... | collective-permute-start | bytes 23048 | tf_op jit(solution)/shard_map/ppermute | solution.py:24
  57.4 13.2 %collective-permute-done.1 = f32[5,4,96,1]{2,1,3,0:T(4,128)} collective-permute-done((f32[5,4,96,1]{2,1,3,0:T(4,128)S(1)}, f32[5,4,96,1]{2,1,3,0:T(4,128)}, u32[]{:S(2)}, u32[]{:S(2)}) %collective-permute-start.1) | collective-permute-done | bytes 7712 | tf_op jit(solution)/shard_map/ppermute | solution.py:24
  72.7 2.0 %copy.84 = f32[5,4,96,1]{3,2,1,0:T(8,128)} copy(f32[5,4,96,1]{2,1,3,0:T(4,128)} %collective-permute-done) | data formatting | bytes 15360 | tf_op jit(solution)/shard_map/ppermute | solution.py:25
  77.3 1.4 rev.6
  79.6 1.4 fusion.74
  81.2 1.3 divide_add_fusion.1
  86.9 5.5 %all-to-all-start.1 = ((f32[64,5,4,128]{3,2,1,0:T(4,128)}), f32[64,5,4,128]{3,2,1,0:T(4,128)}, u32[]{:S(2)}, u32[]{:S(2)}) async-start(f32[64,5,4,128]{3,2,1,0:T(4,128)} %stack.53), calls=%async_computation.1 | async-start | bytes 1310720 | tf_op jit(solution)/shard_map/all_to_all | solution.py:14
  92.4 2.7 %collective-permute-start.7 = (f32[5,4,1,128]{3,2,1,0:T(1,128)S(1)}, f32[5,4,1,128]{3,2,1,0:T(1,128)S(1)}, u32[]{:S(2)}, u32[]{:S(2)}) collective-permute-start(f32[5,4,1,128]{3,2,1,0:T(1,128)S(1)} %get-tuple-element.23), channel_id=1, source_target_pairs={{0,1},{1,2},{2,3},{3,4},{4,5},{5,6},{6,7},{8,9},{9,10},{10,11},{11... | collective-permute-start | bytes 30728 | tf_op jit(solution)/shard_map/ppermute | solution.py:24
  95.8 1.9 %collective-permute-start.5 = (f32[5,4,96,1]{2,1,3,0:T(4,128)S(1)}, f32[5,4,96,1]{2,1,3,0:T(4,128)S(1)}, u32[]{:S(2)}, u32[]{:S(2)}) collective-permute-start(f32[5,4,96,1]{2,1,3,0:T(4,128)S(1)} %copy.92), channel_id=1, source_target_pairs={{0,8},{8,16},{16,24},{24,32},{32,40},{40,48},{48,56},{56,64},{64,7... | collective-permute-start | bytes 23048 | tf_op jit(solution)/shard_map/ppermute | solution.py:24
  98.1 16.6 %collective-permute-start.4 = (f32[5,4,96,1]{2,1,3,0:T(4,128)S(1)}, f32[5,4,96,1]{2,1,3,0:T(4,128)}, u32[]{:S(2)}, u32[]{:S(2)}) collective-permute-start(f32[5,4,96,1]{2,1,3,0:T(4,128)S(1)} %copy.90), channel_id=1, source_target_pairs={{8,0},{16,8},{24,16},{32,24},{40,32},{48,40},{56,48},{64,56},{72,6... | collective-permute-start | bytes 23048 | tf_op jit(solution)/shard_map/ppermute | solution.py:25
  116.5 3.6 %collective-permute-start.6 = (f32[5,4,1,128]{3,2,1,0:T(1,128)}, f32[5,4,1,128]{3,2,1,0:T(1,128)}, u32[]{:S(2)}, u32[]{:S(2)}) collective-permute-start(f32[5,4,1,128]{3,2,1,0:T(1,128)} %get-tuple-element.22), channel_id=1, source_target_pairs={{1,0},{2,1},{3,2},{4,3},{5,4},{6,5},{7,6},{9,8},{10,9},{11,10},{12... | collective-permute-start | bytes 30728 | tf_op jit(solution)/shard_map/ppermute | solution.py:25
  120.0 13.7 %collective-permute-done.5 = f32[5,4,96,1]{2,1,3,0:T(4,128)S(1)} collective-permute-done((f32[5,4,96,1]{2,1,3,0:T(4,128)S(1)}, f32[5,4,96,1]{2,1,3,0:T(4,128)S(1)}, u32[]{:S(2)}, u32[]{:S(2)}) %collective-permute-start.5) | collective-permute-done | bytes 7712 | tf_op jit(solution)/shard_map/ppermute | solution.py:24
  134.1 2.0 %copy.91 = f32[5,4,96,1]{3,2,1,0:T(8,128)} copy(f32[5,4,96,1]{2,1,3,0:T(4,128)} %collective-permute-done.4) | data formatting | bytes 15360 | tf_op jit(solution)/shard_map/ppermute | solution.py:25
  137.3 2.6 %pad_maximum_fusion = (f32[5,4,96,129]{3,2,1,0:T(8,128)}, f32[5,4,96,129]{3,2,1,0:T(8,128)}) fusion(f32[5,4,96,1]{3,2,1,0:T(8,128)S(1)} %copy-done.1, f32[1,4,96,128]{3,2,1,0:T(8,128)S(1)} %get-tuple-element.35, f32[4,4,96,128]{3,2,1,0:T(8,128)S(1)} %fusion.31, f32[5,4,96,1]{3,2,1,0:T(8,128)S(1)} %copy.93), kind=kLoop, calls=%fused_computation.19 | loop fusion | flops 990720 | bytes 2979840 | tf_op jit(solution)/shard_map/concatenate | solution.py:26
  143.7 1.4 rev.7
  146.1 1.3 fusion.84
  148.1 2.6 %divide_add_fusion = f32[4,4,96,128]{3,2,1,0:T(8,128)S(1)} fusion(f32[4,3,96,128]{3,2,1,0:T(8,128)S(1)} %copy-done.22, f32[5,4,1,128]{3,2,1,0:T(1,128)S(1)} %bitcast.140, f32[5,4,95,128]{3,2,1,0:T(8,128)S(1)} %fusion.24, f32[5,4,97,128]{3,2,1,0:T(8,128)S(1)} %copy-done.16, f32[5,4,96,129]{3,2,1,0:T(8,128)} %get-tuple-element.19, ...), kind=kLoop, calls=%fused_computation.86 | loop fusion | flops 6881280 | bytes 7913488 | tf_op jit(solution)/shard_map/add | solution.py:83
  (156 shorter events, 29.1 us)
Async XLA Ops:
  0.6 3.4 %copy-start.3 = (s32[4,96,128]{2,1,0:T(8,128)S(1)}, s32[4,96,128]{2,1,0:T(8,128)}, u32[]{:S(2)}) copy-start(s32[4,96,128]{2,1,0:T(8,128)} %param.18) | copy-start | bytes 589828
  0.6 3.4 %copy-start.45 = (f32[4,96,128]{2,1,0:T(8,128)S(1)}, f32[4,96,128]{2,1,0:T(8,128)}, u32[]{:S(2)}) copy-start(f32[4,96,128]{2,1,0:T(8,128)} %param.17) | copy-start | bytes 589828
  1.8 52.6 %copy-start.5 = (f32[1,4,96,128]{3,2,1,0:T(8,128)}, f32[1,4,96,128]{3,2,1,0:T(8,128)S(1)}, u32[]{:S(2)}) copy-start(f32[1,4,96,128]{3,2,1,0:T(8,128)S(1)} %get-tuple-element.11) | copy-start | bytes 589828
  2.9 51.4 %copy-start.8 = (f32[1,4,96,128]{3,2,1,0:T(8,128)}, f32[1,4,96,128]{3,2,1,0:T(8,128)S(1)}, u32[]{:S(2)}) copy-start(f32[1,4,96,128]{3,2,1,0:T(8,128)S(1)} %get-tuple-element.9) | copy-start | bytes 589828
  6.4 69.1 %all-to-all-start = ((f32[64,5,4,128]{3,2,1,0:T(4,128)}), f32[64,5,4,128]{3,2,1,0:T(4,128)}, u32[]{:S(2)}, u32[]{:S(2)}) async-start(f32[64,5,4,128]{3,2,1,0:T(4,128)} %stack.49), calls=%async_computation | async-start | bytes 1310720 | tf_op jit(solution)/shard_map/all_to_all | solution.py:14
  26.9 47.8 %collective-permute-start.3 = (f32[5,4,1,128]{3,2,1,0:T(1,128)}, f32[5,4,1,128]{3,2,1,0:T(1,128)S(1)}, u32[]{:S(2)}, u32[]{:S(2)}) collective-permute-start(f32[5,4,1,128]{3,2,1,0:T(1,128)} %get-tuple-element.27), channel_id=1, source_target_pairs={{0,1},{1,2},{2,3},{3,4},{4,5},{5,6},{6,7},{8,9},{9,10},{10,11},{11... | collective-permute-start | bytes 30728 | tf_op jit(solution)/shard_map/ppermute | solution.py:24
  29.8 48.8 %collective-permute-start.2 = (f32[5,4,1,128]{3,1,0,2:T(4,128)}, f32[5,4,1,128]{3,1,0,2:T(4,128)}, u32[]{:S(2)}, u32[]{:S(2)}) collective-permute-start(f32[5,4,1,128]{3,1,0,2:T(4,128)} %bitcast.39), channel_id=1, source_target_pairs={{1,0},{2,1},{3,2},{4,3},{5,4},{6,5},{7,6},{9,8},{10,9},{11,10},{12... | collective-permute-start | bytes 30728 | tf_op jit(solution)/shard_map/ppermute | solution.py:25
  34.1 21.1 %copy-start.46 = (f32[3,96,128]{2,1,0:T(8,128)S(1)}, f32[3,96,128]{2,1,0:T(8,128)}, u32[]{:S(2)}) copy-start(f32[3,96,128]{2,1,0:T(8,128)} %param.24) | copy-start | bytes 442372
  36.2 36.4 %collective-permute-start = (f32[5,4,96,1]{2,1,3,0:T(4,128)}, f32[5,4,96,1]{2,1,3,0:T(4,128)}, u32[]{:S(2)}, u32[]{:S(2)}) collective-permute-start(f32[5,4,96,1]{2,1,3,0:T(4,128)} %copy.83), channel_id=1, source_target_pairs={{8,0},{16,8},{24,16},{32,24},{40,32},{48,40},{56,48},{64,56},{72,6... | collective-permute-start | bytes 23048 | tf_op jit(solution)/shard_map/ppermute | solution.py:25
  52.4 18.2 %collective-permute-start.1 = (f32[5,4,96,1]{2,1,3,0:T(4,128)S(1)}, f32[5,4,96,1]{2,1,3,0:T(4,128)}, u32[]{:S(2)}, u32[]{:S(2)}) collective-permute-start(f32[5,4,96,1]{2,1,3,0:T(4,128)S(1)} %copy.85), channel_id=1, source_target_pairs={{0,8},{8,16},{16,24},{24,32},{32,40},{40,48},{48,56},{56,64},{64,7... | collective-permute-start | bytes 23048 | tf_op jit(solution)/shard_map/ppermute | solution.py:24
  86.9 55.0 %all-to-all-start.1 = ((f32[64,5,4,128]{3,2,1,0:T(4,128)}), f32[64,5,4,128]{3,2,1,0:T(4,128)}, u32[]{:S(2)}, u32[]{:S(2)}) async-start(f32[64,5,4,128]{3,2,1,0:T(4,128)} %stack.53), calls=%async_computation.1 | async-start | bytes 1310720 | tf_op jit(solution)/shard_map/all_to_all | solution.py:14
  92.4 47.6 %collective-permute-start.7 = (f32[5,4,1,128]{3,2,1,0:T(1,128)S(1)}, f32[5,4,1,128]{3,2,1,0:T(1,128)S(1)}, u32[]{:S(2)}, u32[]{:S(2)}) collective-permute-start(f32[5,4,1,128]{3,2,1,0:T(1,128)S(1)} %get-tuple-element.23), channel_id=1, source_target_pairs={{0,1},{1,2},{2,3},{3,4},{4,5},{5,6},{6,7},{8,9},{9,10},{10,11},{11... | collective-permute-start | bytes 30728 | tf_op jit(solution)/shard_map/ppermute | solution.py:24
  95.5 20.0 %copy-start.24 = (f32[3,96,128]{2,1,0:T(8,128)S(1)}, f32[3,96,128]{2,1,0:T(8,128)}, u32[]{:S(2)}) copy-start(f32[3,96,128]{2,1,0:T(8,128)} %copy-done.23) | copy-start | bytes 442372
  95.8 37.9 %collective-permute-start.5 = (f32[5,4,96,1]{2,1,3,0:T(4,128)S(1)}, f32[5,4,96,1]{2,1,3,0:T(4,128)S(1)}, u32[]{:S(2)}, u32[]{:S(2)}) collective-permute-start(f32[5,4,96,1]{2,1,3,0:T(4,128)S(1)} %copy.92), channel_id=1, source_target_pairs={{0,8},{8,16},{16,24},{24,32},{32,40},{40,48},{48,56},{56,64},{64,7... | collective-permute-start | bytes 23048 | tf_op jit(solution)/shard_map/ppermute | solution.py:24
  98.1 36.0 %collective-permute-start.4 = (f32[5,4,96,1]{2,1,3,0:T(4,128)S(1)}, f32[5,4,96,1]{2,1,3,0:T(4,128)}, u32[]{:S(2)}, u32[]{:S(2)}) collective-permute-start(f32[5,4,96,1]{2,1,3,0:T(4,128)S(1)} %copy.90), channel_id=1, source_target_pairs={{8,0},{16,8},{24,16},{32,24},{40,32},{48,40},{56,48},{64,56},{72,6... | collective-permute-start | bytes 23048 | tf_op jit(solution)/shard_map/ppermute | solution.py:25
  116.5 28.6 %collective-permute-start.6 = (f32[5,4,1,128]{3,2,1,0:T(1,128)}, f32[5,4,1,128]{3,2,1,0:T(1,128)}, u32[]{:S(2)}, u32[]{:S(2)}) collective-permute-start(f32[5,4,1,128]{3,2,1,0:T(1,128)} %get-tuple-element.22), channel_id=1, source_target_pairs={{1,0},{2,1},{3,2},{4,3},{5,4},{6,5},{7,6},{9,8},{10,9},{11,10},{12... | collective-permute-start | bytes 30728 | tf_op jit(solution)/shard_map/ppermute | solution.py:25
  141.1 4.8 %copy-start.4 = (s32[4,96,128]{2,1,0:T(8,128)S(1)}, s32[4,96,128]{2,1,0:T(8,128)}, u32[]{:S(2)}) copy-start(s32[4,96,128]{2,1,0:T(8,128)} %param.18) | copy-start | bytes 589828
  146.0 2.0 %copy-start.38 = (f32[4,96,128]{2,1,0:T(8,128)S(1)}, f32[4,96,128]{2,1,0:T(8,128)}, u32[]{:S(2)}) copy-start(f32[4,96,128]{2,1,0:T(8,128)} %get-tuple-element.33) | copy-start | bytes 589828
  146.0 2.0 %copy-start.40 = (f32[96,128]{1,0:T(8,128)S(1)}, f32[96,128]{1,0:T(8,128)}, u32[]{:S(2)}) copy-start(f32[96,128]{1,0:T(8,128)} %get-tuple-element.41) | copy-start | bytes 147460
  146.0 2.0 %copy-start.42 = (f32[96,128]{1,0:T(8,128)S(1)}, f32[96,128]{1,0:T(8,128)}, u32[]{:S(2)}) copy-start(f32[96,128]{1,0:T(8,128)} %get-tuple-element.42) | copy-start | bytes 147460
  148.0 2.7 %copy-start.2 = (f32[5,4,96,1]{3,2,1,0:T(8,128)S(1)}, f32[5,4,96,1]{3,2,1,0:T(8,128)}, u32[]{:S(2)}) copy-start(f32[5,4,96,1]{3,2,1,0:T(8,128)} %copy.91) | copy-start | bytes 23044
  148.1 2.7 %copy-start.29 = (f32[1,4,96,128]{3,2,1,0:T(8,128)S(1)}, f32[1,4,96,128]{3,2,1,0:T(8,128)}, u32[]{:S(2)}) copy-start(f32[1,4,96,128]{3,2,1,0:T(8,128)} %reduce-window_subtract_fusion.2) | copy-start | bytes 589828
  148.1 2.7 %copy-start.32 = (s32[96,128]{1,0:T(8,128)S(1)}, s32[96,128]{1,0:T(8,128)}, u32[]{:S(2)}) copy-start(s32[96,128]{1,0:T(8,128)} %param.19) | copy-start | bytes 147460
  148.1 2.7 %copy-start.34 = (f32[96,128]{1,0:T(8,128)S(1)}, f32[96,128]{1,0:T(8,128)}, u32[]{:S(2)}) copy-start(f32[96,128]{1,0:T(8,128)} %param.22) | copy-start | bytes 147460
  (38 other events, 57.4 us)
